TPU v7x, 256 devices: a whole 4x4x8 slice. The times are simulated.
256 devices in a mesh: row: 32 (over z, x), col: 8 (over y, core).
Axes of the slice: x: 4, y: 4, z: 8, core: 2. Of those that a mesh axis runs over, the one named last changes fastest.
Arguments:
- x_points: bfloat16 [32768, 64], P(('row', 'col')), may hold values from -6 to 6
- y_points: bfloat16 [65536, 64], P(('col', 'row')), may hold values from -6 to 6
- row_mass: bfloat16 [32768], P(('row', 'col')), may hold values from 1 to 30, as said below
- col_mass: bfloat16 [65536], P(('col', 'row')), may hold values from 1 to 30, as said below
- multipliers: bfloat16 [32768, 64], P(('row', 'col')), may hold values from -12 to 12
- col_potential: bfloat16 [65536], P(('col', 'row')), may hold values from -3 to 3
- basket: float32 [64], replicated, may hold values from 0.05 to 0.25
- damping: float32 [64], replicated, may hold values from 0.3 to 1.5
Outputs:
- row_potential: float32 [32768], P('row')
- col_potential_new: float32 [65536], P('col')
- multipliers_new: float32 [32768, 64], P(('row', 'col'))
Inputs may be any that keep to these rules, and one draw needn't show every extreme that they name: `row_mass`: weights rise along the points' order by up to a factor of three. `col_mass`: weights rise along the points' order by up to a factor of three.
All inputs are finite; a program needn't handle non-finite values.
Results may differ from a plain program's by a relative error of at most 0.0012.
Values may be sent and summed in bfloat16 or wider, within the bound.
No kernel may reach another device: no remote copies, remote signals or barrier semaphores. Data moves between devices by JAX's collectives and lax.ppermute only.
A program may use at most 64 MiB of HBM per device.

v0:
```python
import jax
import jax.numpy as jnp
from jax import lax
from jax.sharding import PartitionSpec as P

EPS = 0.5
KAPPA = 0.5
RIDGE = 1.0


def merge_lse(parts):
    top = jnp.max(parts, axis=0)
    return top + jnp.log(jnp.sum(jnp.exp(parts - top[None, :]), axis=0))


def on_device(x_points, y_points, row_mass, col_mass, multipliers, col_potential, basket, damping):
    width = x_points.shape[1]
    share = x_points.shape[0]
    x_pack = jnp.concatenate([x_points, multipliers, row_mass[:, None]], axis=1)
    x_rows_pack = lax.all_gather(x_pack, "col", axis=0, tiled=True)
    x_rows = x_rows_pack[:, :width]
    mult_rows = x_rows_pack[:, width : 2 * width]
    mass_rows = x_rows_pack[:, 2 * width]
    ny = y_points.shape[0]
    own_rmass = jnp.zeros((ny,), jnp.bfloat16).at[:share].set(row_mass)
    y_pack = jnp.concatenate(
        [y_points, col_potential[:, None], col_mass[:, None], own_rmass[:, None]], axis=1
    )
    y_cols_pack = lax.all_gather(y_pack, "row", axis=0, tiled=True)
    y_cols = y_cols_pack[:, :width]
    pot_cols = y_cols_pack[:, width].astype(jnp.float32)
    mass_cols = y_cols_pack[:, width + 1].astype(jnp.float32)
    rmass_part = jnp.sum(y_cols_pack[:, width + 2].astype(jnp.float32))
    xf = x_rows.astype(jnp.float32)
    hf = mult_rows.astype(jnp.float32)
    yf = y_cols.astype(jnp.float32)
    row_term2 = 2.0 * (-jnp.sum(hf * xf, axis=1) - KAPPA / width * jnp.sum(xf * xf, axis=1))
    row_basket2 = 2.0 * jnp.sum(xf * basket[None, :], axis=1)
    col_term2 = 2.0 * (-(KAPPA / width) * jnp.sum(yf * yf, axis=1))
    col_basket2 = 2.0 * jnp.sum(yf * basket[None, :], axis=1)
    q_aug = jnp.concatenate([mult_rows * 2, x_rows * (2.0 * KAPPA / width * 2.0)], axis=1)
    y_aug = jnp.concatenate([y_cols, y_cols], axis=1)
    features = jnp.concatenate([yf, yf * yf], axis=1).astype(jnp.bfloat16)
    row_weight = mass_rows.astype(jnp.float32)
    log_row = jnp.log(row_weight)
    log_col = jnp.log(mass_cols)
    nrows = x_rows.shape[0]
    block = min(128, nrows)
    count = nrows // block
    starts = jnp.arange(count, dtype=jnp.int32) * block

    def cut(arr, start):
        return lax.dynamic_slice_in_dim(arr, start, block, 0)

    def block_z(start, row_bias, col_bias):
        dots = jnp.dot(cut(q_aug, start), y_aug.T, preferred_element_type=jnp.float32)
        payoff = jnp.maximum(col_basket2[None, :] - cut(row_basket2, start)[:, None], 0.0)
        return dots + cut(row_bias, start)[:, None] + col_bias[None, :] + payoff

    gshift = col_term2 + pot_cols / EPS + log_col
    zero_rows = jnp.zeros((nrows,), jnp.float32)

    def row_pass(start):
        z = block_z(start, row_term2, gshift)
        top = jnp.max(z, axis=1)
        total = jnp.sum(jnp.exp(z - top[:, None]), axis=1)
        return top + jnp.log(total)

    row_local = lax.map(row_pass, starts).reshape(nrows)
    nu_part = jnp.sum(mass_cols)
    row_msg = jnp.concatenate([row_local, jnp.stack([nu_part, rmass_part])])
    row_all = lax.all_gather(row_msg, "col", axis=0)
    nu_total = jnp.sum(row_all[:, nrows])
    mu_total = jnp.sum(row_all[:, nrows + 1])
    log_nu_total = jnp.log(nu_total)
    row_potential = -EPS * (merge_lse(row_all[:, :nrows]) - log_nu_total)
    fshift = row_term2 + row_potential / EPS + log_row
    zero_cols = jnp.zeros_like(gshift)

    def col_pass(start):
        z = block_z(start, fshift, col_term2)
        top = jnp.max(z, axis=0)
        total = jnp.sum(jnp.exp(z - top[None, :]), axis=0)
        return (top, total)

    col_tops, col_totals = lax.map(col_pass, starts)
    col_top = jnp.max(col_tops, axis=0)
    col_total = jnp.sum(col_totals * jnp.exp(col_tops - col_top[None, :]), axis=0)
    col_local = col_top + jnp.log(col_total)
    col_all = lax.all_gather(col_local, "row", axis=0)
    col_potential_new = -EPS * (merge_lse(col_all) - jnp.log(mu_total))
    gq = col_term2 + col_potential_new / EPS + log_col - log_nu_total
    fq = row_term2 + row_potential / EPS

    def moment_pass(start):
        plan = jnp.exp(block_z(start, fq, gq)).astype(jnp.bfloat16)
        both = jnp.dot(plan, features, preferred_element_type=jnp.float32)
        mass = jnp.sum(plan.astype(jnp.float32), axis=1)
        return jnp.concatenate([both, mass[:, None]], axis=1)

    both = lax.map(moment_pass, starts).reshape(nrows, 2 * width + 1)
    own = lax.psum_scatter(both, "col", scatter_dimension=0, tiled=True)
    first = own[:, :width]
    second = own[:, width : 2 * width]
    own_mass = own[:, 2 * width]
    xo = x_points.astype(jnp.float32)
    grad = first - xo * own_mass[:, None]
    curv = (second - 2.0 * xo * first + xo * xo * own_mass[:, None]) / EPS + RIDGE
    multipliers_new = multipliers.astype(jnp.float32) - damping[None, :] * grad / curv
    return (row_potential, col_potential_new, multipliers_new)


def solution(mesh):
    placed = (
        P(("row", "col"), None),
        P(("col", "row"), None),
        P(("row", "col")),
        P(("col", "row")),
        P(("row", "col"), None),
        P(("col", "row")),
        P(),
        P(),
    )
    return jax.shard_map(
        on_device,
        mesh=mesh,
        in_specs=placed,
        out_specs=(P("row"), P("col"), P(("row", "col"), None)),
        check_vma=False,
    )
```

profile of v0, /device:TPU:4, one launch (start us, length us, event | category | flops | bytes accessed | tf_op | source)
XLA Modules:
  0.0 432.3 jit_solution(2858686389016648679)
XLA Ops:
  12.9 1.3 dynamic-slice.7
  14.9 13.6 %all_gather.16 = bf16[1024,129]{1,0:T(8,128)(2,1)S(1)} all-gather(bf16[128,129]{1,0:T(8,128)(2,1)S(1)} %pad_maximum_fusion.3), channel_id=1, replica_groups=mesh['row'=32,'col'=8] {'col'}, dimensions={0}, use_global_device_ids=true | all-gather | bytes 297216 | tf_op jit(solution)/shard_map/all_gather | solution.py:20
  29.1 1.2 fusion.20
  30.3 60.3 %all-gather.5.cloned.1.call-done = bf16[8192,67]{1,0:T(8,128)(2,1)} async-done(((bf16[256,67]{1,0:T(8,128)(2,1)}), bf16[8192,67]{1,0:T(8,128)(2,1)}) %all-gather.5.cloned.1.call-update) | async-done | bytes 1097744 | tf_op jit(solution)/shard_map/all_gather | solution.py:29
  90.7 4.0 fusion.16
  94.7 3.4 pad_maximum_fusion.1
  98.1 5.0 %convert_reduce_fusion.2 = (f32[]{:T(128)}, f32[]{:T(128)}, f32[8192]{0:T(1024)S(1)}, f32[8192]{0:T(1024)S(1)}) fusion(bf16[8192,67]{1,0:T(8,128)(2,1)S(1)} %copy-done), kind=kLoop, calls=%fused_computation.30 | loop fusion | flops 49150 | bytes 114696 | tf_op jit(solution)/shard_map/reduce_sum | solution.py:33
  103.0 49.9 %while.33 = (s32[]{:T(128)}, f32[8,128]{1,0:T(8,128)S(1)}, s32[8]{0:T(128)S(1)}, bf16[1024,128]{1,0:T(8,128)(2,1)S(1)}, bf16[8192,128]{1,0:T(8,128)(2,1)}, /*ind...) while((s32[]{:T(128)}, f32[8,128]{1,0:T(8,128)S(1)}, ...), condition=%wide.region_8.0_spmd, body=%wide.region_5.8_spmd.sunk | while | flops 276823936 | bytes 10591411 | solution.py:69
  105.7 2.8 fusion.51
  111.9 2.8 fusion.51
  118.1 2.8 fusion.51
  124.4 2.8 fusion.51
  130.6 2.8 fusion.51
  136.8 2.8 fusion.51
  143.1 2.8 fusion.51
  149.3 2.8 fusion.51
  153.0 1.4 concatenate.28
  154.6 24.1 %all-reduce.1 = f32[8208]{0:T(1024)S(1)} all-reduce(f32[8208]{0:T(1024)S(1)} %dynamic-update-slice.3), channel_id=2, replica_groups=mesh['row'=32,'col'=8] {'col'}, use_global_device_ids=true, to_apply=%add.1 | all-reduce | flops 8208 | bytes 65664
  180.8 51.2 %while.34 = (s32[]{:T(128)}, f32[8,8192]{1,0:T(8,128)S(1)}, f32[8,8192]{1,0:T(8,128)S(1)}, s32[8]{0:T(128)S(1)}, bf16[1024,128]{1,0:T(8,128)(2,1)S(1)}, /*index=...) while((s32[]{:T(128)}, f32[8,8192]{1,0:T(8,128)S(1)}, ...), condition=%wide.region_17.18_spmd, body=%wide.region_14.0_spmd.sunk | while | flops 276807680 | bytes 10816703 | solution.py:86
  183.5 2.8 fusion.53
  189.9 2.8 fusion.53
  196.3 2.8 fusion.53
  202.7 2.8 fusion.53
  209.1 2.8 fusion.53
  215.5 2.8 fusion.53
  221.9 2.8 fusion.53
  228.3 2.8 fusion.53
  233.6 71.0 %all-gather.7.cloned.1.call-done = f32[262144]{0:T(1024)} async-done(((f32[8192]{0:T(1024)}), f32[262144]{0:T(1024)}) %all-gather.7.cloned.1.call-update) | async-done | bytes 1048592 | tf_op jit(solution)/shard_map/all_gather | solution.py:90
  304.5 1.4 reshape.99
  306.9 81.9 %while.35 = (s32[]{:T(128)}, f32[8,128,129]{1,0,2:T(8,128)}, s32[8]{0:T(128)S(1)}, bf16[1024,128]{1,0:T(8,128)(2,1)S(1)}, bf16[8192,128]{1,0:T(8,128)(2,1)}, /*i...) while((s32[]{:T(128)}, f32[8,128,129]{1,0,2:T(8,128)}, ...), condition=%wide.region_25.26_spmd, body=%wide.region_23.25_spmd.sunk | while | flops 545275904 | bytes 8952507 | solution.py:101
  309.6 3.2 convert_reduce_fusion.4
  313.8 3.3 dynamic_update_slice.22
  319.8 3.2 convert_reduce_fusion.4
  324.1 3.3 dynamic_update_slice.22
  330.1 3.2 convert_reduce_fusion.4
  334.3 3.3 dynamic_update_slice.22
  340.3 3.2 convert_reduce_fusion.4
  344.6 3.3 dynamic_update_slice.22
  350.6 3.2 convert_reduce_fusion.4
  354.8 3.3 dynamic_update_slice.22
  360.8 3.2 convert_reduce_fusion.4
  365.0 3.3 dynamic_update_slice.22
  371.0 3.2 convert_reduce_fusion.4
  375.3 3.3 dynamic_update_slice.22
  381.3 3.2 convert_reduce_fusion.4
  385.5 3.3 dynamic_update_slice.22
  390.8 32.8 %reduce-scatter.2.cloned.1.call-done = f32[128,129]{0,1:T(8,128)} async-done(((f32[1024,129]{0,1:T(8,128)}), f32[128,129]{0,1:T(8,128)}) %reduce-scatter.2.cloned.1.call-update) | async-done | bytes 66064 | tf_op jit(solution)/shard_map/reduce_scatter | solution.py:102
  424.3 1.5 fusion.26
  (193 shorter events, 52.4 us)
Async XLA Ops:
  7.2 83.5 %all-gather.5.cloned.1.call-start = ((), (), s32[]{:S(2)}) async-start(), calls=%async_computation.1 | async-start | bytes 2162688 | tf_op jit(solution)/shard_map/all_gather | solution.py:29
  11.2 293.4 %all-gather.7.cloned.1.call-start = ((), (), s32[]{:S(2)}) async-start(), calls=%async_computation.3 | async-start | bytes 1081344 | tf_op jit(solution)/shard_map/all_gather | solution.py:90
  90.7 4.0 copy-start
  232.8 190.8 %reduce-scatter.2.cloned.1.call-start = ((), (), s32[]{:S(2)}) async-start(), calls=%async_computation.2 | async-start | bytes 626688 | tf_op jit(solution)/shard_map/reduce_scatter | solution.py:102
  306.9 117.4 %copy-start.1 = (bf16[128,64]{0,1:T(8,128)(2,1)S(1)}, bf16[128,64]{0,1:T(8,128)(2,1)}, u32[]{:S(2)}) copy-start(bf16[128,64]{0,1:T(8,128)(2,1)} %param.20) | copy-start | bytes 49156
  306.9 117.4 %copy-start.2 = (bf16[128,64]{0,1:T(8,128)(2,1)S(1)}, bf16[128,64]{0,1:T(8,128)(2,1)}, u32[]{:S(2)}) copy-start(bf16[128,64]{0,1:T(8,128)(2,1)} %param.16) | copy-start | bytes 49156
  306.9 117.4 %copy-start.3 = (f32[64]{0:T(128)S(1)}, f32[64]{0:T(128)}, u32[]{:S(2)}) copy-start(f32[64]{0:T(128)} %param.23) | copy-start | bytes 772
Sparse Core Ops, SparseCore 0:
  11.3 79.3 all-gather.4
  233.0 71.5 all-gather.6
  391.0 32.6 reduce-scatter.1
where the time goes:
time: 435 us; the launch traced here: 432 us
  waiting for transfers between devices  164 us (38%)
  matrix products  77.7 us (18%)
  local copies, waits for them, and re-layouts  59.4 us (14%)
  loops' own time  46.6 us (11%)
  blocking collectives  37.7 us (9%)
  other arithmetic  30.7 us (7%)
  between operations  16 us (4%)
    all_gather x1, waiting for transfers between devices, on_device(): col_all = lax.all_gather(col_local, 'row', axis=0)  71 us
    dot_general x24, matrix products, block_z(): jnp.dot(cut(q_aug, start), y_aug.T, preferred_element_type=jnp.float32)  69.9 us
    all_gather x1, waiting for transfers between devices, on_device(): y_cols_pack = lax.all_gather(y_pack, 'row', axis=0, tiled=True)  60.3 us
    reduce_scatter x1, waiting for transfers between devices, on_device(): own = lax.psum_scatter(both, 'col', scatter_dimension=0, tiled=True)  32.8 us
    dynamic_update_slice x16, local copies, waits for them, and re-layouts, on_device(): both = lax.map(moment_pass, starts).reshape(nrows, 2 * width + 1)  27.1 us
    unnamed x1, blocking collectives  24.1 us
    another operation x1, loops' own time, on_device(): col_tops, col_totals = lax.map(col_pass, starts)  15.8 us
    another operation x1, loops' own time, on_device(): both = lax.map(moment_pass, starts).reshape(nrows, 2 * width + 1)  15.8 us
  transfers between devices with their start and end apart: 3, of which 3 were waited for; matrix products, arithmetic and copies ran while one was open for 1% of the time, Pallas kernels for 0%

commit v1 on v0

--- a/solution.py
+++ b/solution.py
@@ -6,6 +6,9 @@
 EPS = 0.5
 KAPPA = 0.5
 RIDGE = 1.0
+treat_task = lambda inp, group_axis: jnp.concatenate(
+    lax.all_to_all(jnp.stack([inp] * lax.axis_size(group_axis)), group_axis, 0, 0), axis=0
+)
 
 
 def merge_lse(parts):
@@ -26,7 +29,7 @@
     y_pack = jnp.concatenate(
         [y_points, col_potential[:, None], col_mass[:, None], own_rmass[:, None]], axis=1
     )
-    y_cols_pack = lax.all_gather(y_pack, "row", axis=0, tiled=True)
+    y_cols_pack = treat_task(y_pack, "row")
     y_cols = y_cols_pack[:, :width]
     pot_cols = y_cols_pack[:, width].astype(jnp.float32)
     mass_cols = y_cols_pack[:, width + 1].astype(jnp.float32)

time: 435 us -> 393 us (0.903)
  waiting for transfers between devices: 164 us -> 110 us
  starting transfers between devices: 0.12 us -> 11.8 us
  other arithmetic: 30.7 us -> 20.7 us
  local copies, waits for them, and re-layouts: 59.4 us -> 66.7 us
    all_gather x1 -> x0, waiting for transfers between devices: 60.3 us -> none  [on_device(): y_cols_pack = lax.all_gather(y_pack, 'row', axis=0, tiled=True)]
    all_to_all x0 -> x1, starting transfers between devices: none -> 11.6 us  [lax.all_to_all(jnp.stack([inp] * lax.axis_size(group_axis)), group_axis,...]
    all_to_all x0 -> x1, waiting for transfers between devices: none -> 11.6 us  [lax.all_to_all(jnp.stack([inp] * lax.axis_size(group_axis)), group_axis,...]
    while x0 -> x2, local copies, waits for them, and re-layouts: none -> 5.68 us  [the longest x1 3.22 us: on_device(): both = lax.map(moment_pass, starts).reshape(nrows, 2 * width + 1)]
    all_gather x1, waiting for transfers between devices: 71 us -> 65.9 us  [on_device(): col_all = lax.all_gather(col_local, 'row', axis=0)]
  transfers between devices with their start and end apart: 3 -> 3, of which waited for: 3 -> 3; matrix products, arithmetic and copies ran while one was open for 1% -> 2% of each run, Pallas kernels for 0% -> 0%
where the time goes in v1:
time: 393 us; the launch traced here: 390 us
  waiting for transfers between devices  110 us (28%)
  matrix products  77.8 us (20%)
  local copies, waits for them, and re-layouts  66.7 us (17%)
  loops' own time  48.4 us (12%)
  blocking collectives  38.3 us (10%)
  other arithmetic  20.7 us (5%)
  between operations  16.3 us (4%)
  starting transfers between devices  11.8 us (3%)
    dot_general x24, matrix products, block_z(): jnp.dot(cut(q_aug, start), y_aug.T, preferred_element_type=jnp.float32)  70 us
    all_gather x1, waiting for transfers between devices, on_device(): col_all = lax.all_gather(col_local, 'row', axis=0)  65.9 us
    reduce_scatter x1, waiting for transfers between devices, on_device(): own = lax.psum_scatter(both, 'col', scatter_dimension=0, tiled=True)  32.7 us
    dynamic_update_slice x16, local copies, waits for them, and re-layouts, on_device(): both = lax.map(moment_pass, starts).reshape(nrows, 2 * width + 1)  27 us
    unnamed x1, blocking collectives  24.7 us
    another operation x1, loops' own time, on_device(): row_local = lax.map(row_pass, starts).reshape(nrows)  16.8 us
    another operation x1, loops' own time, on_device(): col_tops, col_totals = lax.map(col_pass, starts)  15.8 us
    another operation x1, loops' own time, on_device(): both = lax.map(moment_pass, starts).reshape(nrows, 2 * width + 1)  15.8 us
  transfers between devices with their start and end apart: 3, of which 3 were waited for; matrix products, arithmetic and copies ran while one was open for 2% of the time, Pallas kernels for 0%

profile of v1, /device:TPU:4, one launch (start us, length us, event | category | flops | bytes accessed | tf_op | source)
XLA Modules:
  0.0 390.2 jit_solution(18299831699002412679)
XLA Ops:
  10.4 11.6 %all-to-all-start = ((bf16[32,256,67]{1,2,0:T(8,128)(2,1)}), bf16[32,256,67]{1,2,0:T(8,128)(2,1)S(1)}, u32[]{:S(2)}, u32[]{:S(2)}) async-start(bf16[32,256,67]{1,2,0:T(8,128)(2,1)} %stack.6), calls=%async_computation | async-start | bytes 2359296 | tf_op jit(solution)/shard_map/all_to_all | solution.py:10
  24.5 1.3 dynamic-slice.7
  26.5 13.6 %all_gather.13 = bf16[1024,129]{1,0:T(8,128)(2,1)S(1)} all-gather(bf16[128,129]{1,0:T(8,128)(2,1)S(1)} %pad_maximum_fusion.3), channel_id=1, replica_groups=mesh['row'=32,'col'=8] {'col'}, dimensions={0}, use_global_device_ids=true | all-gather | bytes 297216 | tf_op jit(solution)/shard_map/all_gather | solution.py:23
  41.3 11.6 %all-to-all-done = bf16[32,256,67]{1,2,0:T(8,128)(2,1)S(1)} async-done(((bf16[32,256,67]{1,2,0:T(8,128)(2,1)}), bf16[32,256,67]{1,2,0:T(8,128)(2,1)S(1)}, u32[]{:S(2)}, u32[]{:S(2)}) %all-to-all-start) | async-done | bytes 1097760 | tf_op jit(solution)/shard_map/all_to_all | solution.py:10
  55.2 1.8 pad_maximum_fusion
  57.0 2.5 copy.49
  59.4 52.2 %while.33 = (s32[]{:T(128)}, f32[8,128]{1,0:T(8,128)S(1)}, s32[8]{0:T(128)S(1)}, bf16[1024,128]{1,0:T(8,128)(2,1)S(1)}, bf16[8192,128]{1,0:T(8,128)(2,1)}, /*ind...) while((s32[]{:T(128)}, f32[8,128]{1,0:T(8,128)S(1)}, ...), condition=%wide.region_8.0_spmd, body=%wide.region_5.8_spmd.sunk | while | flops 276823936 | bytes 10591411 | solution.py:72
  62.3 2.8 fusion.54
  68.9 2.8 fusion.54
  75.4 2.8 fusion.54
  81.9 2.8 fusion.54
  88.5 2.8 fusion.54
  95.0 2.8 fusion.54
  101.5 2.8 fusion.54
  108.0 2.8 fusion.54
  111.7 1.4 concatenate.28
  113.3 24.7 %all-reduce.1 = f32[8208]{0:T(1024)S(1)} all-reduce(f32[8208]{0:T(1024)S(1)} %dynamic-update-slice.3), channel_id=2, replica_groups=mesh['row'=32,'col'=8] {'col'}, use_global_device_ids=true, to_apply=%add.1 | all-reduce | flops 8208 | bytes 65664
  140.1 51.2 %while.34 = (s32[]{:T(128)}, f32[8,8192]{1,0:T(8,128)S(1)}, f32[8,8192]{1,0:T(8,128)S(1)}, s32[8]{0:T(128)S(1)}, bf16[1024,128]{1,0:T(8,128)(2,1)S(1)}, /*index=...) while((s32[]{:T(128)}, f32[8,8192]{1,0:T(8,128)S(1)}, ...), condition=%wide.region_17.18_spmd, body=%wide.region_14.0_spmd.sunk | while | flops 276807680 | bytes 10816703 | solution.py:89
  142.8 2.8 fusion.56
  149.2 2.8 fusion.56
  155.6 2.8 fusion.56
  162.0 2.8 fusion.56
  168.4 2.8 fusion.56
  174.8 2.8 fusion.56
  181.2 2.8 fusion.56
  187.6 2.8 fusion.56
  193.1 3.2 copy.54
  196.3 65.9 %all-gather.4.cloned.1.call-done = f32[262144]{0:T(1024)} async-done(((f32[8192]{0:T(1024)}), f32[262144]{0:T(1024)}) %all-gather.4.cloned.1.call-update) | async-done | bytes 1048592 | tf_op jit(solution)/shard_map/all_gather | solution.py:93
  262.2 1.4 reshape.105
  264.5 82.0 %while.35 = (s32[]{:T(128)}, f32[8,128,129]{1,0,2:T(8,128)}, s32[8]{0:T(128)S(1)}, bf16[1024,128]{1,0:T(8,128)(2,1)}, bf16[8192,128]{1,0:T(8,128)(2,1)}, /*index...) while((s32[]{:T(128)}, f32[8,128,129]{1,0,2:T(8,128)}, ...), condition=%wide.region_25.26_spmd, body=%wide.region_23.25_spmd.sunk | while | flops 545275904 | bytes 8952507 | solution.py:104
  267.2 3.2 convert_reduce_fusion.2
  271.5 3.3 dynamic_update_slice.22
  277.5 3.2 convert_reduce_fusion.2
  281.7 3.3 dynamic_update_slice.22
  287.7 3.2 convert_reduce_fusion.2
  292.0 3.3 dynamic_update_slice.22
  298.0 3.2 convert_reduce_fusion.2
  302.2 3.3 dynamic_update_slice.22
  308.2 3.2 convert_reduce_fusion.2
  312.5 3.3 dynamic_update_slice.22
  318.5 3.2 convert_reduce_fusion.2
  322.7 3.3 dynamic_update_slice.22
  328.7 3.2 convert_reduce_fusion.2
  333.0 3.3 dynamic_update_slice.22
  338.9 3.2 convert_reduce_fusion.2
  343.2 3.3 dynamic_update_slice.22
  348.5 32.7 %reduce-scatter.2.cloned.1.call-done = f32[128,129]{0,1:T(8,128)} async-done(((f32[1024,129]{0,1:T(8,128)}), f32[128,129]{0,1:T(8,128)}) %reduce-scatter.2.cloned.1.call-update) | async-done | bytes 66064 | tf_op jit(solution)/shard_map/reduce_scatter | solution.py:105
  381.9 1.5 fusion.25
  (200 shorter events, 56.0 us)
Async XLA Ops:
  7.2 33.5 %copy-start.3 = (f32[64]{0:T(128)S(1)}, f32[64]{0:T(128)}, u32[]{:S(2)}) copy-start(f32[64]{0:T(128)} %param.22) | copy-start | bytes 772
  10.4 42.5 %all-to-all-start = ((bf16[32,256,67]{1,2,0:T(8,128)(2,1)}), bf16[32,256,67]{1,2,0:T(8,128)(2,1)S(1)}, u32[]{:S(2)}, u32[]{:S(2)}) async-start(bf16[32,256,67]{1,2,0:T(8,128)(2,1)} %stack.6), calls=%async_computation | async-start | bytes 2359296 | tf_op jit(solution)/shard_map/all_to_all | solution.py:10
  22.0 240.2 %all-gather.4.cloned.1.call-start = ((), (), s32[]{:S(2)}) async-start(), calls=%async_computation.3 | async-start | bytes 1081344 | tf_op jit(solution)/shard_map/all_gather | solution.py:93
  191.3 5.0 %copy-start = (bf16[1024,128]{1,0:T(8,128)(2,1)}, bf16[1024,128]{1,0:T(8,128)(2,1)S(1)}, u32[]{:S(2)}) copy-start(bf16[1024,128]{1,0:T(8,128)(2,1)S(1)} %get-tuple-element.659) | copy-start | bytes 786436
  192.1 189.1 %reduce-scatter.2.cloned.1.call-start = ((), (), s32[]{:S(2)}) async-start(), calls=%async_computation.2 | async-start | bytes 626688 | tf_op jit(solution)/shard_map/reduce_scatter | solution.py:105
  264.5 117.3 %copy-start.1 = (bf16[128,64]{0,1:T(8,128)(2,1)S(1)}, bf16[128,64]{0,1:T(8,128)(2,1)}, u32[]{:S(2)}) copy-start(bf16[128,64]{0,1:T(8,128)(2,1)} %param.20) | copy-start | bytes 49156
  264.5 117.3 %copy-start.2 = (bf16[128,64]{0,1:T(8,128)(2,1)S(1)}, bf16[128,64]{0,1:T(8,128)(2,1)}, u32[]{:S(2)}) copy-start(bf16[128,64]{0,1:T(8,128)(2,1)} %param.16) | copy-start | bytes 49156
  264.5 117.3 %copy-start.4 = (f32[64]{0:T(128)S(1)}, f32[64]{0:T(128)}, u32[]{:S(2)}) copy-start(f32[64]{0:T(128)} %param.23) | copy-start | bytes 772
Sparse Core Ops, SparseCore 0:
  192.3 69.8 all-gather.3
  348.6 32.5 reduce-scatter.1
